TPU v7x, 32 devices: a whole 2x2x4 slice. The times are simulated.
32 devices in a mesh: group: 2 (over y), seq: 4 (over z), batch: 2 (over x), chan: 2 (over core).
Axes of the slice: x: 2, y: 2, z: 4, core: 2. Of those that a mesh axis runs over, the one named last changes fastest.
Arguments:
- history: bfloat16 [8, 1024, 4096], P(('group', 'batch'), 'seq', 'chan'), parts along dimension 0, may hold values from -6 to 6
- filter_taps: bfloat16 [1024, 4096], P('seq', 'chan'), may hold values from -0.1875 to 0.1875
- lengths: int32 [8], P(('group', 'batch')), parts along dimension 0, may hold values from 256 to 1024, as said below
- inner_gate: bfloat16 [8, 256, 4096], P(('group', 'batch'), 'seq', 'chan'), parts along dimension 0, may hold values from -6 to 6
- values_in: bfloat16 [8, 256, 4096], P(('group', 'batch'), 'seq', 'chan'), parts along dimension 0, may hold values from -6 to 6
- outer_gate: bfloat16 [8, 256, 4096], P(('group', 'batch'), 'seq', 'chan'), parts along dimension 0, may hold values from -6 to 6
- skip_gain: float32 [4096], P('chan'), may hold values from -4 to 4
Outputs:
- mixed: bfloat16 [8, 256, 4096], P(('group', 'batch'), 'seq', 'chan'), parts along dimension 0
- next_history: bfloat16 [8, 1024, 4096], P(('group', 'batch'), 'seq', 'chan'), parts along dimension 0
There are 2 independent parts, one for each index of `group`. A program takes and returns all parts, laid end to end along the dimension named above; an argument that names none is the same for every part. Nothing has to cross between parts.
Inputs may be any that keep to these rules, and one draw needn't show every extreme that they name: `lengths`: each request's prefilled length is a multiple of 256; some request of every part has exactly 1024, and some other is shorter.
All inputs are finite; a program needn't handle non-finite values.
Results may differ from a plain program's by a relative error of at most 0.0044.
Values may be sent and summed in bfloat16 or wider, within the bound.
No kernel may reach another device: no remote copies, remote signals or barrier semaphores. Data moves between devices by JAX's collectives and lax.ppermute only.
A program may use at most 128 MiB of HBM per device.

v0:
```python
import jax
import jax.numpy as jnp
from jax import lax
from jax.sharding import PartitionSpec as P


def from_behind(block, axis, distance):
    devices = range(lax.axis_size(axis))
    route = [(i - distance, i) for i in devices if i - distance in devices]
    return lax.ppermute(block, axis, route)


def correlate(signal, kernel):
    width = signal.shape[2]
    return lax.conv_general_dilated(
        signal,
        kernel[:, None, :],
        (1,),
        "VALID",
        dimension_numbers=("NWC", "WIO", "NWC"),
        feature_group_count=width,
        preferred_element_type=jnp.float32,
    )


def recent_term(product_all, front_lags, start, count):
    requests, span_len, width = product_all.shape
    padded = jnp.concatenate(
        [jnp.zeros((requests, span_len, width), jnp.bfloat16), product_all], axis=1
    )
    window = lax.dynamic_slice_in_dim(padded, start + 1, count + span_len - 1, 1)
    reversed_front = front_lags[::-1]
    return correlate(window, reversed_front)


def per_device(history, filter_taps, lengths, inner_gate, values_in, outer_gate, skip_gain):
    position = lax.axis_index("seq")
    requests, tile_len, width = history.shape
    own_tokens = inner_gate.shape[1]
    span_len = own_tokens * lax.axis_size("seq")
    product_own = (inner_gate.astype(jnp.float32) * values_in.astype(jnp.float32)).astype(
        jnp.bfloat16
    )
    product_all = lax.all_gather(product_own, "seq", axis=1, tiled=True)
    lag_ids = position * tile_len + jnp.arange(tile_len, dtype=jnp.int32)
    live_rows = jnp.where(
        (lag_ids[None, :] < lengths[:, None])[:, :, None], history, jnp.zeros_like(history)
    )
    older_tail = from_behind(history, "seq", 1)
    following = from_behind(filter_taps, "seq", -1)
    segment = jnp.concatenate([filter_taps, following], axis=0)[1:]

    def per_request(kernel_rows):
        return correlate(segment[None], kernel_rows)[0]

    hist_term = jax.vmap(per_request)(live_rows)
    first_term = lax.cond(
        position == 0,
        lambda: recent_term(product_all, filter_taps, 0, span_len),
        lambda: jnp.zeros((requests, span_len, width), jnp.float32),
    )
    partial_sum = jnp.moveaxis(hist_term + first_term, 1, 0)
    summed = jnp.moveaxis(
        lax.psum_scatter(
            lax.slice_in_dim(partial_sum, 0, own_tokens * lax.axis_size("seq"), axis=0),
            "seq",
            scatter_dimension=0,
            tiled=True,
        ),
        0,
        1,
    )
    product_float = product_own.astype(jnp.float32)
    total = summed + skip_gain[None, None, :] * product_float
    mixed = (outer_gate.astype(jnp.float32) * total).astype(jnp.bfloat16)
    head_rows = jnp.where(position == 0, product_all[:, ::-1], older_tail)
    next_history = jnp.concatenate([head_rows, history[:, : tile_len - span_len]], axis=1)
    return (mixed, next_history)


def solution(mesh):
    in_specs = (
        P(("group", "batch"), "seq", "chan"),
        P("seq", "chan"),
        P(("group", "batch")),
        P(("group", "batch"), "seq", "chan"),
        P(("group", "batch"), "seq", "chan"),
        P(("group", "batch"), "seq", "chan"),
        P("chan"),
    )
    out_specs = (P(("group", "batch"), "seq", "chan"), P(("group", "batch"), "seq", "chan"))
    return jax.shard_map(
        per_device, mesh=mesh, in_specs=in_specs, out_specs=out_specs, check_vma=False
    )
```

profile of v0, /device:TPU:0, one launch (start us, length us, event | category | flops | bytes accessed | tf_op | source)
XLA Modules:
  0.0 501.3 jit_solution(14019448444654914452)
XLA Ops:
  7.2 1.4 collective-permute-start
  8.7 1.3 multiply_convert_fusion
  10.0 0.8 copy-done.2
  10.8 1.3 copy.38
  12.1 0.0 all-reduce.3.cloned.1.call-start
  12.2 0.1 broadcast_compare_fusion
  12.3 0.2 select_bitcast_fusion
  12.5 42.7 %collective-permute-done = bf16[256,2048]{1,0:T(8,128)(2,1)S(1)} collective-permute-done((bf16[256,2048]{1,0:T(8,128)(2,1)}, bf16[256,2048]{1,0:T(8,128)(2,1)S(1)}, u32[]{:S(2)}, u32[]{:S(2)}) %collective-permute-start) | collective-permute-done | bytes 1048608 | tf_op jit(solution)/shard_map/ppermute | solution.py:10
  55.3 0.5 fusion.5
  55.8 108.7 %convolution_bitcast_fusion = f32[2,1,256,2048]{3,1,0,2:T(1,128)} fusion(bf16[256,1,2048,2]{2,0,3,1:T(8,128)(2,1)S(1)} %select_bitcast_fusion, bf16[1,511,2048,1]{2,1,3,0:T(8,128)(2,1)S(1)} %fusion.5), kind=kOutput, calls=%fused_computation.2 | convolution fusion | flops 536870912 | bytes 8384512 | tf_op jit(solution)/shard_map/convolution
  164.5 123.7 %conditional.1 = (f32[2,256,2048]{2,0,1:T(2,128)}) conditional(s32[]{:T(128)} %convert_element_type.22, () %tuple.14, (bf16[256,2048]{1,0:T(8,128)(2,1)S(1)}, bf16[2,256,2048]{2,0,1:T(2,128)(2,1)}) %tuple.27), branch_computations={%region_0.1_spmd, %region_1.2_spmd} | conditional | flops 269484032 | bytes 17825828 | solution.py:57
  164.5 10.2 %rev.4 = bf16[256,2048]{1,0:T(8,128)(2,1)} reverse(bf16[256,2048]{1,0:T(8,128)(2,1)S(1)} %get-tuple-element.8), dimensions={0} | reverse | bytes 2097152 | tf_op jit(solution)/shard_map/cond/branch_1_fun/rev | solution.py:32
  174.8 113.4 %fusion = f32[2,256,2048]{2,0,1:T(2,128)} fusion(bf16[2,256,2048]{2,0,1:T(2,128)(2,1)S(1)} %copy-done.6, bf16[256,1,2048]{2,0,1:T(8,128)(2,1)} %bitcast.31), kind=kOutput, calls=%fused_computation | convolution fusion | flops 269484032 | bytes 7340032 | tf_op jit(solution)/shard_map/cond/branch_1_fun/conv_general_dilated | solution.py:15
  288.2 8.8 %fusion.2 = f32[256,2,2048]{2,1,0:T(2,128)} fusion(f32[2,256,2048]{2,0,1:T(2,128)} %get-tuple-element.19, f32[2,1,256,2048]{3,1,0,2:T(1,128)} %convolution_bitcast_fusion), kind=kLoop, calls=%fused_computation.4 | loop fusion | flops 1048576 | bytes 12582912 | tf_op jit(solution)/shard_map/transpose | solution.py:62
  297.0 1.6 copy-done.1
  298.6 3.5 copy.40
  302.0 1.4 collective-permute-start.1
  303.5 0.6 dynamic-slice
  304.7 87.6 %collective-permute-done.1 = bf16[2,256,2048]{2,0,1:T(2,128)(2,1)S(1)} collective-permute-done((bf16[2,256,2048]{2,0,1:T(2,128)(2,1)}, bf16[2,256,2048]{2,0,1:T(2,128)(2,1)S(1)}, u32[]{:S(2)}, u32[]{:S(2)}) %collective-permute-start.1) | collective-permute-done | bytes 2097184 | tf_op jit(solution)/shard_map/ppermute | solution.py:10
  392.3 3.8 broadcast_select_fusion
  396.1 2.2 copy.41
  398.3 93.3 %all-reduce.3.cloned.1.call-done = f32[256,2,2048]{2,1,0:T(2,128)} async-done(((f32[256,2,2048]{2,1,0:T(2,128)}), f32[256,2,2048]{2,1,0:T(2,128)}) %all-reduce.3.cloned.1.call-update) | async-done | bytes 4194320
  491.6 1.3 constant_dynamic-slice_fusion
  492.9 1.5 fusion.7
  (25 shorter events, 0.1 us)
Async XLA Ops:
  7.2 5.1 %copy-start.9 = (s32[2]{0:T(128)S(1)}, s32[2]{0:T(128)}, u32[]{:S(2)}) copy-start(s32[2]{0:T(128)} %param.11) | copy-start | bytes 28
  7.2 5.1 %copy-start = (bf16[2,256,2048]{2,1,0:T(8,128)(2,1)S(1)}, bf16[2,256,2048]{2,1,0:T(8,128)(2,1)}, u32[]{:S(2)}) copy-start(bf16[2,256,2048]{2,1,0:T(8,128)(2,1)} %param.9) | copy-start | bytes 6291460
  7.2 157.3 %all-gather.2.cloned.1.call-start = ((), (), s32[]{:S(2)}) async-start(), calls=%async_computation | async-start | bytes 2621440 | tf_op jit(solution)/shard_map/all_gather | solution.py:44
  7.2 48.0 %collective-permute-start = (bf16[256,2048]{1,0:T(8,128)(2,1)}, bf16[256,2048]{1,0:T(8,128)(2,1)S(1)}, u32[]{:S(2)}, u32[]{:S(2)}) collective-permute-start(bf16[256,2048]{1,0:T(8,128)(2,1)} %param.10), channel_id=1, source_target_pairs={{4,0},{8,4},{12,8},{5,1},{9,5},{13,9},{6,2},{10,6},{14,10},{7,3},{... | collective-permute-start | bytes 3145736 | tf_op jit(solution)/shard_map/ppermute | solution.py:10
  10.0 0.8 copy-start.2
  12.1 479.5 %all-reduce.3.cloned.1.call-start = ((), (), s32[]{:S(2)}) async-start(), calls=%async_computation.1 | async-start | bytes 8388608
  12.3 43.0 %copy-start.4 = (bf16[256,2048]{1,0:T(8,128)(2,1)S(1)}, bf16[256,2048]{1,0:T(8,128)(2,1)}, u32[]{:S(2)}) copy-start(bf16[256,2048]{1,0:T(8,128)(2,1)} %param.10) | copy-start | bytes 3145732
  55.8 108.7 %copy-start.5 = (bf16[256,2048]{1,0:T(8,128)(2,1)S(1)}, bf16[256,2048]{1,0:T(8,128)(2,1)}, u32[]{:S(2)}) copy-start(bf16[256,2048]{1,0:T(8,128)(2,1)} %param.10) | copy-start | bytes 3145732
  164.5 10.3 %copy-start.6 = (bf16[2,256,2048]{2,0,1:T(2,128)(2,1)S(1)}, bf16[2,256,2048]{2,0,1:T(2,128)(2,1)}, u32[]{:S(2)}) copy-start(bf16[2,256,2048]{2,0,1:T(2,128)(2,1)} %get-tuple-element.4) | copy-start | bytes 6291460 | tf_op jit(solution)/shard_map/cond
  297.0 1.6 copy-start.1
  298.6 4.9 copy-start.10
  302.0 90.3 %collective-permute-start.1 = (bf16[2,256,2048]{2,0,1:T(2,128)(2,1)}, bf16[2,256,2048]{2,0,1:T(2,128)(2,1)S(1)}, u32[]{:S(2)}, u32[]{:S(2)}) collective-permute-start(bf16[2,256,2048]{2,0,1:T(2,128)(2,1)} %copy.40), channel_id=1, source_target_pairs={{0,4},{4,8},{8,12},{1,5},{5,9},{9,13},{2,6},{6,10},{10,14},{3,7},{... | collective-permute-start | bytes 6291464 | tf_op jit(solution)/shard_map/ppermute | solution.py:10
  398.3 94.6 %copy-start.3 = (bf16[2,64,2048]{2,1,0:T(8,128)(2,1)S(1)}, bf16[2,64,2048]{2,1,0:T(8,128)(2,1)}, u32[]{:S(2)}) copy-start(bf16[2,64,2048]{2,1,0:T(8,128)(2,1)} %copy-done.2) | copy-start | bytes 1572868
  398.3 94.6 %copy-start.7 = (bf16[2,64,2048]{2,1,0:T(8,128)(2,1)S(1)}, bf16[2,64,2048]{2,1,0:T(8,128)(2,1)}, u32[]{:S(2)}) copy-start(bf16[2,64,2048]{2,1,0:T(8,128)(2,1)} %param.14) | copy-start | bytes 1572868
  398.3 94.6 %copy-start.8 = (f32[2048]{0:T(1024)S(1)}, f32[2048]{0:T(1024)}, u32[]{:S(2)}) copy-start(f32[2048]{0:T(1024)} %param.15) | copy-start | bytes 24580
Sparse Core Ops, SparseCore 0:
  12.3 58.7 all-gather.1
  297.1 194.4 all-reduce.2
where the time goes:
time: 502 us; the launch traced here: 501 us
  waiting for transfers between devices  224 us (45%)
  matrix products  222 us (44%)
  local copies, waits for them, and re-layouts  21.5 us (4%)
  other arithmetic  16.1 us (3%)
  between operations  14.8 us (3%)
    ppermute x2, waiting for transfers between devices, from_behind(): return lax.ppermute(block, axis, route)  130 us
    conv_general_dilated x1, matrix products, correlate(): lax.conv_general_dilated(signal, kernel[:, None, :], (1,), 'VALID', dimen...  113 us
    another operation x1, matrix products  109 us
    unnamed x3, waiting for transfers between devices  93.3 us
    rev x1, local copies, waits for them, and re-layouts, recent_term(): reversed_front = front_lags[::-1]  10.2 us
  transfers between devices with their start and end apart: 4, of which 3 were waited for; matrix products, arithmetic and copies ran while one was open for 24% of the time, Pallas kernels for 0%

commit v1 on v0

v1 whole, which is shorter than its diff:
```python
import jax
import jax.numpy as jnp
from jax import lax
from jax.sharding import PartitionSpec as P


def from_behind(block, axis, distance):
    devices = range(lax.axis_size(axis))
    route = [(i - distance, i) for i in devices if i - distance in devices]
    return lax.ppermute(block, axis, route)


def correlate(signal, kernel):
    width = signal.shape[2]
    return lax.conv_general_dilated(
        signal,
        kernel[:, None, :],
        (1,),
        "VALID",
        dimension_numbers=("NWC", "WIO", "NWC"),
        feature_group_count=width,
        preferred_element_type=jnp.float32,
    )


def per_device(history, filter_taps, lengths, inner_gate, values_in, outer_gate, skip_gain):
    position = lax.axis_index("seq")
    n_seq = lax.axis_size("seq")
    requests, tile_len, width = history.shape
    own_tokens = inner_gate.shape[1]
    span_len = own_tokens * n_seq
    assert span_len == tile_len
    step = own_tokens
    product_own = (inner_gate.astype(jnp.float32) * values_in.astype(jnp.float32)).astype(
        jnp.bfloat16
    )
    product_all = lax.all_gather(product_own, "seq", axis=1, tiled=True)
    head_product = product_all[:, ::-1]
    row_ids = position * tile_len + jnp.arange(tile_len, dtype=jnp.int32)
    live_rows = jnp.where(
        (row_ids[None, :] < lengths[:, None])[:, :, None], history, jnp.zeros_like(history)
    )
    prev_keep = ((row_ids - tile_len)[None, :] < lengths[:, None])[:, :, None]

    head_parts = []
    prev_live = []
    sums = []
    for c in range(n_seq):
        lo = tile_len - step * (c + 1)
        hi = lo + step
        sent = from_behind(history[:, lo:hi], "seq", 1)
        if c == 0:
            first = product_own[:, ::-1]
        else:
            first = head_product[:, lo:hi]
        head_c = jnp.where(position == 0, first, sent)
        head_parts.append(head_c)
        prev_live.insert(
            0, jnp.where(prev_keep[:, lo:hi], head_c, jnp.zeros_like(head_c))
        )
        segment = jnp.concatenate(prev_live + [live_rows[:, : hi - 1]], axis=1)
        partial_rev = correlate(segment, filter_taps)
        sums.append(lax.psum(partial_rev, "seq"))
    own_rev = jnp.stack(sums)[position]
    summed = own_rev[:, ::-1]
    product_float = product_own.astype(jnp.float32)
    total = summed + skip_gain[None, None, :] * product_float
    mixed = (outer_gate.astype(jnp.float32) * total).astype(jnp.bfloat16)
    next_history = jnp.concatenate(head_parts[::-1], axis=1)
    return (mixed, next_history)


def solution(mesh):
    in_specs = (
        P(("group", "batch"), "seq", "chan"),
        P("seq", "chan"),
        P(("group", "batch")),
        P(("group", "batch"), "seq", "chan"),
        P(("group", "batch"), "seq", "chan"),
        P(("group", "batch"), "seq", "chan"),
        P("chan"),
    )
    out_specs = (P(("group", "batch"), "seq", "chan"), P(("group", "batch"), "seq", "chan"))
    return jax.shard_map(
        per_device, mesh=mesh, in_specs=in_specs, out_specs=out_specs, check_vma=False
    )
```

time: 502 us -> 417 us (0.83)
  matrix products: 222 us -> 103 us
  local copies, waits for them, and re-layouts: 21.5 us -> 58.5 us
  waiting for transfers between devices: 224 us -> 203 us
  starting transfers between devices: 2.91 us -> 14.9 us
    psum x0 -> x1, waiting for transfers between devices: none -> 155 us  [per_device(): sums.append(lax.psum(partial_rev, 'seq'))]
    ppermute x2 -> x4, waiting for transfers between devices: 130 us -> 0.01 us  [from_behind(): return lax.ppermute(block, axis, route)]
    another operation x1 -> x0, matrix products: 109 us -> none
    unnamed x3 -> x2, waiting for transfers between devices: 93.3 us -> 0.03 us
    all_gather x1, waiting for transfers between devices: 0.01 us -> 48.2 us  [per_device(): product_all = lax.all_gather(product_own, 'seq', axis=1, tiled=True)]
    slice x0 -> x7, local copies, waits for them, and re-layouts: none -> 34 us  [the longest x4 28.7 us: per_device(): first = head_product[:, lo:hi]]
    ppermute x2 -> x4, starting transfers between devices: 2.83 us -> 14.8 us  [from_behind(): return lax.ppermute(block, axis, route)]
    conv_general_dilated x1 -> x4, matrix products: 113 us -> 103 us  [correlate(): lax.conv_general_dilated(signal, kernel[:, None, :], (1,), 'VALID', dimen...]
  transfers between devices with their start and end apart: 4 -> 6, of which waited for: 3 -> 2; matrix products, arithmetic and copies ran while one was open for 24% -> 14% of each run, Pallas kernels for 0% -> 0%
where the time goes in v1:
time: 417 us; the launch traced here: 413 us
  waiting for transfers between devices  203 us (49%)
  matrix products  103 us (25%)
  local copies, waits for them, and re-layouts  58.5 us (14%)
  other arithmetic  18.6 us (4%)
  starting transfers between devices  14.9 us (4%)
  between operations  14.2 us (3%)
    psum x1, waiting for transfers between devices, per_device(): sums.append(lax.psum(partial_rev, 'seq'))  155 us
    conv_general_dilated x4, matrix products, correlate(): lax.conv_general_dilated(signal, kernel[:, None, :], (1,), 'VALID', dimen...  103 us
    all_gather x1, waiting for transfers between devices, per_device(): product_all = lax.all_gather(product_own, 'seq', axis=1, tiled=True)  48.2 us
    slice x4, local copies, waits for them, and re-layouts, per_device(): first = head_product[:, lo:hi]  28.7 us
    ppermute x4, starting transfers between devices, from_behind(): return lax.ppermute(block, axis, route)  14.8 us
    rev x1, local copies, waits for them, and re-layouts, per_device(): first = product_own[:, ::-1]  8.36 us
  transfers between devices with their start and end apart: 6, of which 2 were waited for; matrix products, arithmetic and copies ran while one was open for 14% of the time, Pallas kernels for 0%

profile of v1, /device:TPU:0, one launch (start us, length us, event | category | flops | bytes accessed | tf_op | source)
XLA Modules:
  0.0 412.6 jit_solution(7550243576826798161)
XLA Ops:
  10.1 2.9 fusion.27
  12.9 5.7 %collective-permute-start = (bf16[2,64,2048]{2,1,0:T(8,128)(2,1)}, bf16[2,64,2048]{2,1,0:T(8,128)(2,1)}, u32[]{:S(2)}, u32[]{:S(2)}) collective-permute-start(bf16[2,64,2048]{2,1,0:T(8,128)(2,1)} %get-tuple-element.21), channel_id=1, source_target_pairs={{0,4},{4,8},{8,12},{1,5},{5,9},{9,13},{2,6},{6,10},{10,14},{3,7},{... | collective-permute-start | bytes 1572872 | tf_op jit(solution)/shard_map/ppermute | solution.py:10
  18.7 3.5 collective-permute-start.1
  22.2 3.5 collective-permute-start.3
  25.7 2.1 collective-permute-start.2
  27.9 1.8 broadcast_select_fusion
  29.8 8.4 %rev.7 = bf16[2,64,2048]{2,1,0:T(8,128)(2,1)} reverse(bf16[2,64,2048]{2,1,0:T(8,128)(2,1)} %copy-done.1), dimensions={1} | reverse | bytes 1048576 | tf_op jit(solution)/shard_map/rev | solution.py:53
  40.6 48.2 %all-gather.2.cloned.1.call-done = bf16[2,256,2048]{2,0,1:T(2,128)(2,1)} async-done(((bf16[2,64,2048]{2,0,1:T(2,128)(2,1)}), bf16[2,256,2048]{2,0,1:T(2,128)(2,1)}) %all-gather.2.cloned.1.call-update) | async-done | bytes 2097168 | tf_op jit(solution)/shard_map/all_gather | solution.py:37
  88.8 3.7 fusion.28
  93.5 8.3 %slice.69 = bf16[2,64,2048]{2,1,0:T(8,128)(2,1)} reverse(bf16[2,64,2048]{2,1,0:T(8,128)(2,1)} %copy.60), dimensions={1} | reverse | bytes 1048576 | tf_op jit(solution)/shard_map/slice | solution.py:55
  101.8 2.2 select_dynamic-update-slice_fusion
  104.0 2.0 copy.59
  106.0 8.3 %slice.64 = bf16[2,64,2048]{2,1,0:T(8,128)(2,1)} reverse(bf16[2,64,2048]{2,1,0:T(8,128)(2,1)} %copy.59), dimensions={1} | reverse | bytes 1048576 | tf_op jit(solution)/shard_map/slice | solution.py:55
  114.3 2.4 constant_dynamic-update-slice_fusion.2
  117.7 8.3 %slice.59 = bf16[2,64,2048]{2,1,0:T(8,128)(2,1)} reverse(bf16[2,64,2048]{2,1,0:T(8,128)(2,1)} %copy.58), dimensions={1} | reverse | bytes 1048576 | tf_op jit(solution)/shard_map/slice | solution.py:55
  126.1 2.3 constant_dynamic-update-slice_fusion.1
  130.5 27.0 %fusion.17 = f32[1,2,64,2048]{3,1,2,0:T(2,128)} fusion(bf16[2,319,2048]{2,1,0:T(8,128)(2,1)} %slice_dynamic-update-slice_fusion, bf16[256,1,2048]{2,0,1:T(8,128)(2,1)S(1)} %bitcast.22), kind=kOutput, calls=%fused_computation.18 | convolution fusion | flops 134217728 | bytes 4710400 | tf_op jit(solution)/shard_map/conv_general_dilated | solution.py:15
  158.6 25.6 %fusion.11 = f32[1,2,64,2048]{3,1,2,0:T(2,128)} fusion(bf16[2,319,2048]{2,1,0:T(8,128)(2,1)S(1)} %get-tuple-element.28, bf16[256,1,2048]{2,0,1:T(8,128)(2,1)S(1)} %bitcast.24), kind=kOutput, calls=%fused_computation.16 | convolution fusion | flops 134217728 | bytes 4710400 | tf_op jit(solution)/shard_map/conv_general_dilated | solution.py:15
  184.2 25.5 %fusion.14 = f32[1,2,64,2048]{3,1,2,0:T(2,128)} fusion(bf16[2,319,2048]{2,1,0:T(8,128)(2,1)S(1)} %get-tuple-element.29, bf16[256,1,2048]{2,0,1:T(8,128)(2,1)S(1)} %bitcast.23), kind=kOutput, calls=%fused_computation.17 | convolution fusion | flops 134217728 | bytes 4710400 | tf_op jit(solution)/shard_map/conv_general_dilated | solution.py:15
  209.7 25.5 %fusion.8 = f32[1,2,64,2048]{3,1,2,0:T(2,128)} fusion(bf16[2,319,2048]{2,1,0:T(8,128)(2,1)S(1)} %get-tuple-element.30, bf16[256,1,2048]{2,0,1:T(8,128)(2,1)S(1)} %bitcast.21), kind=kOutput, calls=%fused_computation.15 | convolution fusion | flops 134217728 | bytes 4710400 | tf_op jit(solution)/shard_map/conv_general_dilated | solution.py:15
  238.2 154.7 %all-reduce.3.cloned.1.call-done = (f32[1,2,64,2048]{3,1,2,0:T(2,128)}, f32[1,2,64,2048]{3,1,2,0:T(2,128)}, f32[1,2,64,2048]{3,1,2,0:T(2,128)}, f32[1,2,64,2048]{3,1,2,0:T(2,128)}) async-done(((f32[1,2,64,2048]{3,1,2,0:T(2,128)}, f32[1,2,64,2048]{3,1,2,0:T(2,128)}, f32[1,2,64,2048]{3,1,2,0:T(2,128)}, f32[1,2,64,2048]{3,1,2,0:T(2,128)}), (f32[1,2,64,2048]{3,1,2,0:T(2,128)}, f32[1,2,64,2048]{3,1,2,0:T(2,128)}, ...) | async-done | bytes 4194320 | tf_op jit(solution)/shard_map/psum | solution.py:63
  392.9 3.3 fusion.22
  396.3 1.6 copy.86
  397.9 6.8 %rev.8 = f32[2,64,2048]{2,1,0:T(8,128)S(1)} reverse(f32[2,64,2048]{2,1,0:T(8,128)} %bitcast.26), dimensions={1} | reverse | bytes 2097152 | tf_op jit(solution)/shard_map/rev | solution.py:65
  (53 shorter events, 14.7 us)
Async XLA Ops:
  7.2 123.4 %copy-start = (bf16[256,2048]{1,0:T(8,128)(2,1)S(1)}, bf16[256,2048]{1,0:T(8,128)(2,1)}, u32[]{:S(2)}) copy-start(bf16[256,2048]{1,0:T(8,128)(2,1)} %param.8) | copy-start | bytes 3145732
  7.2 81.6 %all-gather.2.cloned.1.call-start = ((), (), s32[]{:S(2)}) async-start(), calls=%async_computation | async-start | bytes 2621440 | tf_op jit(solution)/shard_map/all_gather | solution.py:37
  8.6 19.2 %copy-start.1 = (bf16[2,64,2048]{2,1,0:T(8,128)(2,1)}, bf16[2,64,2048]{2,1,0:T(8,128)(2,1)S(1)}, u32[]{:S(2)}) copy-start(bf16[2,64,2048]{2,1,0:T(8,128)(2,1)S(1)} %multiply_convert_fusion.1) | copy-start | bytes 1572868
  10.0 17.8 %copy-start.14 = (s32[2]{0:T(128)S(1)}, s32[2]{0:T(128)}, u32[]{:S(2)}) copy-start(s32[2]{0:T(128)} %param.9) | copy-start | bytes 28
  10.0 382.9 %all-reduce.3.cloned.1.call-start = ((), (), s32[]{:S(2)}) async-start(), calls=%async_computation.1 | async-start | bytes 8388608 | tf_op jit(solution)/shard_map/psum | solution.py:63
  12.9 115.5 %collective-permute-start = (bf16[2,64,2048]{2,1,0:T(8,128)(2,1)}, bf16[2,64,2048]{2,1,0:T(8,128)(2,1)}, u32[]{:S(2)}, u32[]{:S(2)}) collective-permute-start(bf16[2,64,2048]{2,1,0:T(8,128)(2,1)} %get-tuple-element.21), channel_id=1, source_target_pairs={{0,4},{4,8},{8,12},{1,5},{5,9},{9,13},{2,6},{6,10},{10,14},{3,7},{... | collective-permute-start | bytes 1572872 | tf_op jit(solution)/shard_map/ppermute | solution.py:10
  18.7 107.4 %collective-permute-start.1 = (bf16[2,64,2048]{2,1,0:T(8,128)(2,1)}, bf16[2,64,2048]{2,1,0:T(8,128)(2,1)}, u32[]{:S(2)}, u32[]{:S(2)}) collective-permute-start(bf16[2,64,2048]{2,1,0:T(8,128)(2,1)} %get-tuple-element.22), channel_id=1, source_target_pairs={{0,4},{4,8},{8,12},{1,5},{5,9},{9,13},{2,6},{6,10},{10,14},{3,7},{... | collective-permute-start | bytes 1572872 | tf_op jit(solution)/shard_map/ppermute | solution.py:10
  22.2 79.6 %collective-permute-start.3 = (bf16[2,64,2048]{2,1,0:T(8,128)(2,1)}, bf16[2,64,2048]{2,1,0:T(8,128)(2,1)}, u32[]{:S(2)}, u32[]{:S(2)}) collective-permute-start(bf16[2,64,2048]{2,1,0:T(8,128)(2,1)} %get-tuple-element.23), channel_id=1, source_target_pairs={{0,4},{4,8},{8,12},{1,5},{5,9},{9,13},{2,6},{6,10},{10,14},{3,7},{... | collective-permute-start | bytes 1572872 | tf_op jit(solution)/shard_map/ppermute | solution.py:10
  25.7 88.7 %collective-permute-start.2 = (bf16[2,64,2048]{2,1,0:T(8,128)(2,1)}, bf16[2,64,2048]{2,1,0:T(8,128)(2,1)}, u32[]{:S(2)}, u32[]{:S(2)}) collective-permute-start(bf16[2,64,2048]{2,1,0:T(8,128)(2,1)} %get-tuple-element.24), channel_id=1, source_target_pairs={{0,4},{4,8},{8,12},{1,5},{5,9},{9,13},{2,6},{6,10},{10,14},{3,7},{... | collective-permute-start | bytes 1572872 | tf_op jit(solution)/shard_map/ppermute | solution.py:10
  114.3 2.5 copy-start.7
  126.1 2.3 copy-start.6
  130.5 27.0 %copy-start.3 = (bf16[2,191,2048]{2,1,0:T(8,128)(2,1)S(1)}, bf16[2,191,2048]{2,1,0:T(8,128)(2,1)}, u32[]{:S(2)}) copy-start(bf16[2,191,2048]{2,1,0:T(8,128)(2,1)} %slice.76) | copy-start | bytes 4694020
  130.5 27.0 %copy-start.4 = (bf16[2,127,2048]{2,1,0:T(8,128)(2,1)S(1)}, bf16[2,127,2048]{2,1,0:T(8,128)(2,1)}, u32[]{:S(2)}) copy-start(bf16[2,127,2048]{2,1,0:T(8,128)(2,1)} %slice.79) | copy-start | bytes 3121156
  130.5 27.0 %copy-start.5 = (bf16[2,64,2048]{2,1,0:T(8,128)(2,1)S(1)}, bf16[2,64,2048]{2,1,0:T(8,128)(2,1)}, u32[]{:S(2)}) copy-start(bf16[2,64,2048]{2,1,0:T(8,128)(2,1)} %get-tuple-element.17) | copy-start | bytes 1572868
  235.1 1.0 copy-start.8
  235.1 1.2 copy-start.9
  235.1 1.4 copy-start.10
  235.1 1.5 copy-start.11
  396.3 8.5 %copy-start.2 = (bf16[2,64,2048]{2,1,0:T(8,128)(2,1)S(1)}, bf16[2,64,2048]{2,1,0:T(8,128)(2,1)}, u32[]{:S(2)}) copy-start(bf16[2,64,2048]{2,1,0:T(8,128)(2,1)} %copy-done.1) | copy-start | bytes 1572868
  396.3 8.5 %copy-start.12 = (bf16[2,64,2048]{2,1,0:T(8,128)(2,1)S(1)}, bf16[2,64,2048]{2,1,0:T(8,128)(2,1)}, u32[]{:S(2)}) copy-start(bf16[2,64,2048]{2,1,0:T(8,128)(2,1)} %param.12) | copy-start | bytes 1572868
  396.3 8.5 %copy-start.13 = (f32[2048]{0:T(1024)S(1)}, f32[2048]{0:T(1024)}, u32[]{:S(2)}) copy-start(f32[2048]{0:T(1024)} %param.13) | copy-start | bytes 24580
Sparse Core Ops, SparseCore 0:
  10.2 78.5 all-gather.1
  235.3 157.6 all-reduce.2

commit v2 on v1

--- a/solution.py
+++ b/solution.py
@@ -34,8 +34,9 @@
     product_own = (inner_gate.astype(jnp.float32) * values_in.astype(jnp.float32)).astype(
         jnp.bfloat16
     )
-    product_all = lax.all_gather(product_own, "seq", axis=1, tiled=True)
-    head_product = product_all[:, ::-1]
+    product_rev = (
+        inner_gate[:, ::-1].astype(jnp.float32) * values_in[:, ::-1].astype(jnp.float32)
+    ).astype(jnp.bfloat16)
     row_ids = position * tile_len + jnp.arange(tile_len, dtype=jnp.int32)
     live_rows = jnp.where(
         (row_ids[None, :] < lengths[:, None])[:, :, None], history, jnp.zeros_like(history)
@@ -50,9 +51,11 @@
         hi = lo + step
         sent = from_behind(history[:, lo:hi], "seq", 1)
         if c == 0:
-            first = product_own[:, ::-1]
+            first = product_rev
         else:
-            first = head_product[:, lo:hi]
+            first = lax.ppermute(product_rev, "seq", [(c, 0)])
+        if sums:
+            (sent, first), _ = lax.optimization_barrier(((sent, first), last_partial))
         head_c = jnp.where(position == 0, first, sent)
         head_parts.append(head_c)
         prev_live.insert(
@@ -60,6 +63,9 @@
         )
         segment = jnp.concatenate(prev_live + [live_rows[:, : hi - 1]], axis=1)
         partial_rev = correlate(segment, filter_taps)
+        last_partial = partial_rev
+        if sums:
+            partial_rev, _ = lax.optimization_barrier((partial_rev, sums[-1]))
         sums.append(lax.psum(partial_rev, "seq"))
     own_rev = jnp.stack(sums)[position]
     summed = own_rev[:, ::-1]

time: 417 us -> 328 us (0.79)
  waiting for transfers between devices: 203 us -> 123 us
  local copies, waits for them, and re-layouts: 58.5 us -> 24.2 us
  other arithmetic: 18.6 us -> 46.1 us
  starting transfers between devices: 14.9 us -> 19.3 us
    all_gather x1 -> x0, waiting for transfers between devices: 48.2 us -> none  [per_device(): product_all = lax.all_gather(product_own, 'seq', axis=1, tiled=True)]
    psum x1 -> x4, waiting for transfers between devices: 155 us -> 123 us  [per_device(): sums.append(lax.psum(partial_rev, 'seq'))]
    slice x4 -> x0, local copies, waits for them, and re-layouts: 28.7 us -> none  [per_device(): first = head_product[:, lo:hi]]
    conv_general_dilated x0 -> x2, other arithmetic: none -> 21.8 us  [correlate(): lax.conv_general_dilated(signal, kernel[:, None, :], (1,), 'VALID', dimen...]
    unnamed x33 -> x40, local copies, waits for them, and re-layouts: 5.53 us -> 19.1 us
    select_n x0 -> x3, other arithmetic: none -> 8.48 us  [per_device(): jnp.where(prev_keep[:, lo:hi], head_c, jnp.zeros_like(head_c))]
    rev x1 -> x0, local copies, waits for them, and re-layouts: 8.36 us -> none  [per_device(): first = product_own[:, ::-1]]
    rev x1, local copies, waits for them, and re-layouts: 6.83 us -> 0.45 us  [per_device(): summed = own_rev[:, ::-1]]
  transfers between devices with their start and end apart: 6 -> 11, of which waited for: 2 -> 3; matrix products, arithmetic and copies ran while one was open for 14% -> 49% of each run, Pallas kernels for 0% -> 0%
where the time goes in v2:
time: 328 us; the launch traced here: 327 us
  waiting for transfers between devices  123 us (38%)
  matrix products  100 us (30%)
  other arithmetic  46.1 us (14%)
  local copies, waits for them, and re-layouts  24.2 us (7%)
  starting transfers between devices  19.3 us (6%)
  between operations  14.1 us (4%)
    psum x4, waiting for transfers between devices, per_device(): sums.append(lax.psum(partial_rev, 'seq'))  123 us
    conv_general_dilated x4, matrix products, correlate(): lax.conv_general_dilated(signal, kernel[:, None, :], (1,), 'VALID', dimen...  100 us
    conv_general_dilated x2, other arithmetic, correlate(): lax.conv_general_dilated(signal, kernel[:, None, :], (1,), 'VALID', dimen...  21.8 us
    unnamed x40, local copies, waits for them, and re-layouts  19.1 us
    ppermute x4, starting transfers between devices, from_behind(): return lax.ppermute(block, axis, route)  14.8 us
    select_n x3, other arithmetic, per_device(): jnp.where(prev_keep[:, lo:hi], head_c, jnp.zeros_like(head_c))  8.48 us
  transfers between devices with their start and end apart: 11, of which 3 were waited for; matrix products, arithmetic and copies ran while one was open for 49% of the time, Pallas kernels for 0%

profile of v2, /device:TPU:0, one launch (start us, length us, event | category | flops | bytes accessed | tf_op | source)
XLA Modules:
  0.0 327.2 jit_solution(1952499923579106428)
XLA Ops:
  10.3 5.8 %collective-permute-start.5 = (bf16[2,64,2048]{2,0,1:T(2,128)(2,1)}, bf16[2,64,2048]{2,0,1:T(2,128)(2,1)}, u32[]{:S(2)}, u32[]{:S(2)}) collective-permute-start(bf16[2,64,2048]{2,0,1:T(2,128)(2,1)} %copy.52), channel_id=1, source_target_pairs={{0,4},{4,8},{8,12},{1,5},{5,9},{9,13},{2,6},{6,10},{10,14},{3,7},{... | collective-permute-start | bytes 1572872 | tf_op jit(solution)/shard_map/ppermute | solution.py:10
  17.4 3.5 %collective-permute-start = (bf16[2,64,2048]{2,0,1:T(2,128)(2,1)}, bf16[2,64,2048]{2,0,1:T(2,128)(2,1)}, u32[]{:S(2)}, u32[]{:S(2)}) collective-permute-start(bf16[2,64,2048]{2,0,1:T(2,128)(2,1)} %copy.53), channel_id=1, source_target_pairs={{0,4},{4,8},{8,12},{1,5},{5,9},{9,13},{2,6},{6,10},{10,14},{3,7},{... | collective-permute-start | bytes 1572872 | tf_op jit(solution)/shard_map/ppermute | solution.py:10
  22.2 3.5 %collective-permute-start.1 = (bf16[2,64,2048]{2,0,1:T(2,128)(2,1)}, bf16[2,64,2048]{2,0,1:T(2,128)(2,1)}, u32[]{:S(2)}, u32[]{:S(2)}) collective-permute-start(bf16[2,64,2048]{2,0,1:T(2,128)(2,1)} %copy.54), channel_id=1, source_target_pairs={{0,4},{4,8},{8,12},{1,5},{5,9},{9,13},{2,6},{6,10},{10,14},{3,7},{... | collective-permute-start | bytes 1572872 | tf_op jit(solution)/shard_map/ppermute | solution.py:10
  29.3 5.0 %broadcast_select_fusion = bf16[2,256,2048]{2,0,1:T(2,128)(2,1)S(1)} fusion(pred[2,256]{0,1:T(8,128)(4,1)S(1)} %broadcast_compare_fusion, bf16[2,256,2048]{2,1,0:T(8,128)(2,1)} %param.7), kind=kLoop, calls=%fused_computation.4 | loop fusion | flops 1048576 | bytes 4194816 | tf_op jit(solution)/shard_map/jit(_where)/select_n | solution.py:41
  40.2 2.7 broadcast_select_fusion.8
  45.5 23.9 %fusion = f32[2,64,2048]{2,0,1:T(2,128)} fusion(bf16[2,255,2048]{2,0,1:T(2,128)(2,1)S(1)} %slice-done.2, bf16[2,64,2048]{2,0,1:T(2,128)(2,1)S(1)} %get-tuple-element.30, bf16[256,1,2048]{2,0,1:T(8,128)(2,1)S(1)} %bitcast.19), kind=kOutput, calls=%fused_computation.5 | convolution fusion | flops 139444224 | bytes 4710400 | tf_op jit(solution)/shard_map/conv_general_dilated | solution.py:15
  71.1 2.8 broadcast_select_fusion.3
  73.9 9.5 %fusion.41 = bf16[2,319,2048]{2,0,1:T(2,128)(2,1)S(1)} fusion(bf16[2,191,2048]{2,0,1:T(2,128)(2,1)S(1)} %slice-done.1, bf16[2,64,2048]{2,0,1:T(2,128)(2,1)} %copy-done.4, bf16[2,64,2048]{2,0,1:T(2,128)(2,1)S(1)} %get-tuple-element.28), kind=kLoop, calls=%fused_computation.10.clone.1 | loop fusion | flops 2613248 | bytes 5226496 | tf_op jit(solution)/shard_map/conv_general_dilated | solution.py:15
  83.4 25.4 %fusion.4 = f32[2,64,2048]{2,0,1:T(2,128)} fusion(bf16[256,1,2048]{2,0,1:T(8,128)(2,1)S(1)} %bitcast.22, bf16[2,319,2048]{2,0,1:T(2,128)(2,1)S(1)} %fusion.41), kind=kOutput, calls=%fused_computation.9 | convolution fusion | flops 134217728 | bytes 4710400 | tf_op jit(solution)/shard_map/conv_general_dilated | solution.py:15
  108.9 2.9 broadcast_select_fusion.2
  111.8 12.3 %fusion.43 = bf16[2,319,2048]{2,0,1:T(2,128)(2,1)S(1)} fusion(bf16[2,127,2048]{2,0,1:T(2,128)(2,1)S(1)} %slice-done, bf16[2,64,2048]{2,0,1:T(2,128)(2,1)S(1)} %copy-done.5, bf16[2,64,2048]{2,0,1:T(2,128)(2,1)S(1)} %get-tuple-element.28, bf16[2,64,2048]{2,0,1:T(2,128)(2,1)S(1)} %get-tuple-element.26), kind=kLoop, calls=%fused_computation.16.clone.1 | loop fusion | flops 3919872 | bytes 5226496 | tf_op jit(solution)/shard_map/conv_general_dilated | solution.py:15
  124.1 25.4 %fusion.10 = f32[2,64,2048]{2,0,1:T(2,128)} fusion(bf16[256,1,2048]{2,0,1:T(8,128)(2,1)S(1)} %bitcast.21, bf16[2,319,2048]{2,0,1:T(2,128)(2,1)S(1)} %fusion.43), kind=kOutput, calls=%fused_computation.15 | convolution fusion | flops 134217728 | bytes 4710400 | tf_op jit(solution)/shard_map/conv_general_dilated | solution.py:15
  149.6 3.0 fusion.26
  152.9 2.3 constant_dynamic-update-slice_fusion.2
  155.2 2.2 constant_dynamic-update-slice_fusion.1
  157.4 2.2 constant_dynamic-update-slice_fusion
  160.8 47.0 %all-reduce.7.cloned.1.call-done = f32[2,64,2048]{2,0,1:T(2,128)} async-done(((f32[2,64,2048]{2,0,1:T(2,128)}), f32[2,64,2048]{2,0,1:T(2,128)}) %all-reduce.7.cloned.1.call-update) | async-done | bytes 1048592 | tf_op jit(solution)/shard_map/psum | solution.py:69
  207.9 25.4 %fusion.21 = f32[2,64,2048]{2,0,1:T(2,128)} fusion(bf16[2,319,2048]{2,0,1:T(2,128)(2,1)} %slice_dynamic-update-slice_fusion, bf16[256,1,2048]{2,0,1:T(8,128)(2,1)S(1)} %bitcast.20), kind=kOutput, calls=%fused_computation.39 | convolution fusion | flops 134217728 | bytes 4710400 | tf_op jit(solution)/shard_map/conv_general_dilated | solution.py:15
  233.3 28.1 %all-reduce.9.cloned.1.call-done = f32[2,64,2048]{2,0,1:T(2,128)} async-done(((f32[2,64,2048]{2,0,1:T(2,128)}), f32[2,64,2048]{2,0,1:T(2,128)}) %all-reduce.9.cloned.1.call-update) | async-done | bytes 1048592 | tf_op jit(solution)/shard_map/psum | solution.py:69
  261.5 3.1 pad_maximum_fusion
  264.6 2.2 copy.41
  266.9 48.2 %all-reduce.11.cloned.1.call-done = f32[1,2,64,2048]{3,1,2,0:T(2,128)} async-done(((f32[1,2,64,2048]{3,1,2,0:T(2,128)}), f32[1,2,64,2048]{3,1,2,0:T(2,128)}) %all-reduce.11.cloned.1.call-update) | async-done | bytes 1048592 | tf_op jit(solution)/shard_map/psum | solution.py:69
  315.0 2.1 fusion.20
  318.2 2.4 multiply_convert_fusion
  (75 shorter events, 22.1 us)
Async XLA Ops:
  7.2 38.3 %copy-start = (bf16[256,2048]{1,0:T(8,128)(2,1)S(1)}, bf16[256,2048]{1,0:T(8,128)(2,1)}, u32[]{:S(2)}) copy-start(bf16[256,2048]{1,0:T(8,128)(2,1)} %param.8) | copy-start | bytes 3145732
  7.2 145.4 %all-reduce.5.cloned.1.call-start = ((), (), s32[]{:S(2)}) async-start(), calls=%async_computation | async-start | bytes 2097152 | tf_op jit(solution)/shard_map/psum | solution.py:69
  9.0 20.2 %copy-start.14 = (s32[2]{0:T(128)S(1)}, s32[2]{0:T(128)}, u32[]{:S(2)}) copy-start(s32[2]{0:T(128)} %param.9) | copy-start | bytes 28
  10.3 139.2 %collective-permute-start.5 = (bf16[2,64,2048]{2,0,1:T(2,128)(2,1)}, bf16[2,64,2048]{2,0,1:T(2,128)(2,1)}, u32[]{:S(2)}, u32[]{:S(2)}) collective-permute-start(bf16[2,64,2048]{2,0,1:T(2,128)(2,1)} %copy.52), channel_id=1, source_target_pairs={{0,4},{4,8},{8,12},{1,5},{5,9},{9,13},{2,6},{6,10},{10,14},{3,7},{... | collective-permute-start | bytes 1572872 | tf_op jit(solution)/shard_map/ppermute | solution.py:10
  17.4 22.8 %collective-permute-start = (bf16[2,64,2048]{2,0,1:T(2,128)(2,1)}, bf16[2,64,2048]{2,0,1:T(2,128)(2,1)}, u32[]{:S(2)}, u32[]{:S(2)}) collective-permute-start(bf16[2,64,2048]{2,0,1:T(2,128)(2,1)} %copy.53), channel_id=1, source_target_pairs={{0,4},{4,8},{8,12},{1,5},{5,9},{9,13},{2,6},{6,10},{10,14},{3,7},{... | collective-permute-start | bytes 1572872 | tf_op jit(solution)/shard_map/ppermute | solution.py:10
  22.2 47.2 %collective-permute-start.1 = (bf16[2,64,2048]{2,0,1:T(2,128)(2,1)}, bf16[2,64,2048]{2,0,1:T(2,128)(2,1)}, u32[]{:S(2)}, u32[]{:S(2)}) collective-permute-start(bf16[2,64,2048]{2,0,1:T(2,128)(2,1)} %copy.54), channel_id=1, source_target_pairs={{0,4},{4,8},{8,12},{1,5},{5,9},{9,13},{2,6},{6,10},{10,14},{3,7},{... | collective-permute-start | bytes 1572872 | tf_op jit(solution)/shard_map/ppermute | solution.py:10
  27.1 81.7 %collective-permute-start.3 = (bf16[2,64,2048]{2,0,1:T(2,128)(2,1)}, bf16[2,64,2048]{2,0,1:T(2,128)(2,1)}, u32[]{:S(2)}, u32[]{:S(2)}) collective-permute-start(bf16[2,64,2048]{2,0,1:T(2,128)(2,1)} %copy.55), channel_id=1, source_target_pairs={{0,4},{4,8},{8,12},{1,5},{5,9},{9,13},{2,6},{6,10},{10,14},{3,7},{... | collective-permute-start | bytes 1572872 | tf_op jit(solution)/shard_map/ppermute | solution.py:10
  36.8 8.7 %slice-start.2 = ((bf16[2,256,2048]{2,0,1:T(2,128)(2,1)}), bf16[2,255,2048]{2,0,1:T(2,128)(2,1)S(1)}, s32[]{:S(2)}) async-start(bf16[2,256,2048]{2,0,1:T(2,128)(2,1)} %copy-done.1), calls=%async_computation.6 | async-start | bytes 4177920 | tf_op jit(solution)/shard_map/slice | solution.py:64
  42.9 65.9 %collective-permute-start.4 = (bf16[2,64,2048]{2,0,1:T(2,128)(2,1)}, bf16[2,64,2048]{2,0,1:T(2,128)(2,1)}, u32[]{:S(2)}, u32[]{:S(2)}) collective-permute-start(bf16[2,64,2048]{2,0,1:T(2,128)(2,1)} %get-tuple-element.32), channel_id=1, source_target_pairs={{8,0},{9,1},{10,2},{11,3},{24,16},{25,17},{26,18},{27,19}} | collective-permute-start | bytes 1572872 | tf_op jit(solution)/shard_map/ppermute | solution.py:56
  44.2 26.6 %collective-permute-start.2 = (bf16[2,64,2048]{2,0,1:T(2,128)(2,1)}, bf16[2,64,2048]{2,0,1:T(2,128)(2,1)}, u32[]{:S(2)}, u32[]{:S(2)}) collective-permute-start(bf16[2,64,2048]{2,0,1:T(2,128)(2,1)} %get-tuple-element.32), channel_id=1, source_target_pairs={{4,0},{5,1},{6,2},{7,3},{20,16},{21,17},{22,18},{23,19}} | collective-permute-start | bytes 1572872 | tf_op jit(solution)/shard_map/ppermute | solution.py:56
  69.4 80.1 %collective-permute-start.6 = (bf16[2,64,2048]{2,0,1:T(2,128)(2,1)}, bf16[2,64,2048]{2,0,1:T(2,128)(2,1)}, u32[]{:S(2)}, u32[]{:S(2)}) collective-permute-start(bf16[2,64,2048]{2,0,1:T(2,128)(2,1)} %get-tuple-element.32), channel_id=1, source_target_pairs={{12,0},{13,1},{14,2},{15,3},{28,16},{29,17},{30,18},{31,19}} | collective-permute-start | bytes 1572872 | tf_op jit(solution)/shard_map/ppermute | solution.py:56
  70.9 136.9 %all-reduce.7.cloned.1.call-start = ((), (), s32[]{:S(2)}) async-start(), calls=%async_computation.1 | async-start | bytes 2097152 | tf_op jit(solution)/shard_map/psum | solution.py:69
  73.9 37.9 %copy-start.3 = (bf16[2,64,2048]{2,0,1:T(2,128)(2,1)}, bf16[2,64,2048]{2,0,1:T(2,128)(2,1)S(1)}, u32[]{:S(2)}) copy-start(bf16[2,64,2048]{2,0,1:T(2,128)(2,1)S(1)} %get-tuple-element.28) | copy-start | bytes 1572868
  83.4 28.4 %copy-start.5 = (bf16[2,64,2048]{2,0,1:T(2,128)(2,1)S(1)}, bf16[2,64,2048]{2,0,1:T(2,128)(2,1)}, u32[]{:S(2)}) copy-start(bf16[2,64,2048]{2,0,1:T(2,128)(2,1)} %copy-done.4) | copy-start | bytes 1572868
  111.8 12.3 %copy-start.6 = (bf16[2,64,2048]{2,0,1:T(2,128)(2,1)}, bf16[2,64,2048]{2,0,1:T(2,128)(2,1)S(1)}, u32[]{:S(2)}) copy-start(bf16[2,64,2048]{2,0,1:T(2,128)(2,1)S(1)} %get-tuple-element.26) | copy-start | bytes 1572868
  124.1 25.5 %copy-start.12 = (pred[2,64]{0,1:T(8,128)(4,1)S(1)}, pred[2,64]{0,1:T(8,128)(4,1)}, u32[]{:S(2)}) copy-start(pred[2,64]{0,1:T(8,128)(4,1)} %copy.37) | copy-start | bytes 388
  152.6 7.0 %copy-start.2 = (bf16[2,256,2048]{2,0,1:T(2,128)(2,1)S(1)}, bf16[2,256,2048]{2,0,1:T(2,128)(2,1)}, u32[]{:S(2)}) copy-start(bf16[2,256,2048]{2,0,1:T(2,128)(2,1)} %copy-done.1) | copy-start | bytes 6291460
  152.6 108.8 %all-reduce.9.cloned.1.call-start = ((), (), s32[]{:S(2)}) async-start(), calls=%async_computation.2 | async-start | bytes 2097152 | tf_op jit(solution)/shard_map/psum | solution.py:69
  207.8 53.6 %copy-start.7 = (bf16[2,64,2048]{2,0,1:T(2,128)(2,1)S(1)}, bf16[2,64,2048]{2,0,1:T(2,128)(2,1)}, u32[]{:S(2)}) copy-start(bf16[2,64,2048]{2,0,1:T(2,128)(2,1)} %get-tuple-element.29) | copy-start | bytes 1572868
  207.9 53.6 %copy-start.8 = (bf16[2,64,2048]{2,0,1:T(2,128)(2,1)S(1)}, bf16[2,64,2048]{2,0,1:T(2,128)(2,1)}, u32[]{:S(2)}) copy-start(bf16[2,64,2048]{2,0,1:T(2,128)(2,1)} %get-tuple-element.27) | copy-start | bytes 1572868
  207.9 53.6 %copy-start.9 = (bf16[2,64,2048]{2,0,1:T(2,128)(2,1)S(1)}, bf16[2,64,2048]{2,0,1:T(2,128)(2,1)}, u32[]{:S(2)}) copy-start(bf16[2,64,2048]{2,0,1:T(2,128)(2,1)} %get-tuple-element.25) | copy-start | bytes 1572868
  207.9 53.6 %copy-start.10 = (bf16[2,64,2048]{2,0,1:T(2,128)(2,1)S(1)}, bf16[2,64,2048]{2,0,1:T(2,128)(2,1)}, u32[]{:S(2)}) copy-start(bf16[2,64,2048]{2,0,1:T(2,128)(2,1)} %get-tuple-element.31) | copy-start | bytes 1572868
  207.9 107.1 %all-reduce.11.cloned.1.call-start = ((), (), s32[]{:S(2)}) async-start(), calls=%async_computation.3 | async-start | bytes 2097152 | tf_op jit(solution)/shard_map/psum | solution.py:69
  264.6 50.4 %copy-start.11 = (f32[2,64,2048]{2,0,1:T(2,128)S(1)}, f32[2,64,2048]{2,0,1:T(2,128)}, u32[]{:S(2)}) copy-start(f32[2,64,2048]{2,0,1:T(2,128)} %all-reduce.5.cloned.1.call-done) | copy-start | bytes 3145732
  (5 other events, 12.5 us)
Sparse Core Ops, SparseCore 0:
  71.0 57.9 all-reduce.4
  152.7 55.0 all-reduce.6
  210.2 51.1 all-reduce.8
  263.8 51.1 all-reduce.10
